TPU v7x, 32 devices: a whole 2x2x4 slice. The times are simulated.
32 devices in a mesh: stn: 16 (over z, x, core), chan: 2 (over y).
Axes of the slice: x: 2, y: 2, z: 4, core: 2. Of those that a mesh axis runs over, the one named last changes fastest.
Arguments:
- screen: float32 [32, 512, 512], P('stn'), may hold values from -6 to 6
- pierce_coords: float32 [2, 16, 2, 16, 1024], P(None, 'stn', 'chan'), may hold values from 0 to 1
- query_dest: int32 [16, 2, 16, 1024], P('stn', 'chan'), may hold values from 0 to 4096, as said below
- positions: float32 [3, 256], P(None, 'stn'), may hold values from -50 to 50
- directions: float32 [3, 512], replicated, may hold values from -0.7 to 0.7
- freq_ratio: float32 [64], P('chan'), may hold values from 0.7 to 1.4
- source_flux: float32 [512], replicated, may hold values from 0.2 to 5
- spectral_index: float32 [512], replicated, may hold values from -1.5 to 0.5
Outputs:
- visibilities: float32 [64, 2, 256, 256], P('chan', None, 'stn')
Inputs may be any that keep to these rules, and one draw needn't show every extreme that they name: `query_dest`: in each block every number 0 to 4095 appears in exactly one slot and empty slots hold 4096; an owner's live slots come first in its row; one owner, the same for every block, has all 1024 of its slots live in every block.
All inputs are finite; a program needn't handle non-finite values.
Results may differ from a plain program's by a relative error of at most 0.008.
Values may be sent and summed in bfloat16 or wider, within the bound.
No kernel may reach another device: no remote copies, remote signals or barrier semaphores. Data moves between devices by JAX's collectives and lax.ppermute only.
A program may use at most 128 MiB of HBM per device.

v0:
```python
import math
import jax
import jax.numpy as jnp
from jax import lax
from jax.sharding import PartitionSpec as P

TWO_PI = 2.0 * math.pi


def interpolate(values, coords, strip_rows, tile_cols):
    row_pos = coords[0] * (strip_rows - 1)
    col_pos = coords[1] * (tile_cols - 1)
    row_low = jnp.clip(jnp.floor(row_pos), 0.0, strip_rows - 2.0)
    col_low = jnp.clip(jnp.floor(col_pos), 0.0, tile_cols - 2.0)
    frac_y = row_pos - row_low
    frac_x = col_pos - col_low
    corner = row_low.astype(jnp.int32) * tile_cols + col_low.astype(jnp.int32)
    lower_pair = (1.0 - frac_x) * values[corner] + frac_x * values[corner + 1]
    upper_pair = (1.0 - frac_x) * values[corner + tile_cols] + frac_x * values[
        corner + tile_cols + 1
    ]
    return (1.0 - frac_y) * lower_pair + frac_y * upper_pair


def make_phasors(station_rows, iono_rows, directions, freq_ratio):
    delays = (
        station_rows[:, 0:1] * directions[0][None, :]
        + station_rows[:, 1:2] * directions[1][None, :]
    )
    delays = delays + station_rows[:, 2:3] * directions[2][None, :]
    angles = (TWO_PI * freq_ratio)[None, :, None] * delays[:, None, :] + iono_rows[
        :, None, :
    ] / freq_ratio[None, :, None]
    return jnp.concatenate([jnp.cos(angles), jnp.sin(angles)], axis=-1).astype(jnp.bfloat16)


def spectrum(source_flux, spectral_index, freq_ratio, count):
    return (
        source_flux[None, :]
        * jnp.exp(spectral_index[None, :] * jnp.log(freq_ratio)[:, None])
        / math.sqrt(count)
    )


def weight_rows(phasors, intensity):
    sources = intensity.shape[1]
    real_part = (phasors[:, :, :sources].astype(jnp.float32) * intensity[None]).astype(jnp.bfloat16)
    imag_part = (phasors[:, :, sources:].astype(jnp.float32) * intensity[None]).astype(jnp.bfloat16)
    upper_rows = jnp.concatenate([real_part, imag_part], axis=-1)
    lower_rows = jnp.concatenate([imag_part, -real_part], axis=-1)
    return jnp.concatenate([upper_rows, lower_rows], axis=0)


def body(
    screen,
    pierce_coords,
    query_dest,
    positions,
    directions,
    freq_ratio,
    source_flux,
    spectral_index,
):
    groups = lax.axis_size("stn")
    tile_cols = screen.shape[2]
    strip_rows = screen.shape[0] * screen.shape[1]
    values = screen.reshape(-1)
    capacity = query_dest.shape[3]
    coords = pierce_coords.reshape(2, groups, capacity)
    sampled = interpolate(
        values,
        lax.all_to_all(coords, "stn", split_axis=1, concat_axis=1, tiled=True),
        strip_rows,
        tile_cols,
    )
    returned = lax.all_to_all(sampled, "stn", split_axis=0, concat_axis=0, tiled=True)
    stations_local = positions.shape[1]
    local_sources = source_flux.shape[0] // lax.axis_size("chan")
    queries = stations_local * local_sources
    buffer = (
        jnp.zeros((queries + 1,), jnp.float32).at[query_dest.reshape(-1)].set(returned.reshape(-1))
    )
    own_iono = buffer[:queries].reshape(stations_local, local_sources)
    iono_phase = lax.all_gather(own_iono, "chan", axis=1, tiled=True)
    station_rows = positions.T
    own_phasors = make_phasors(station_rows, iono_phase, directions, freq_ratio)
    intensity = spectrum(source_flux, spectral_index, freq_ratio, source_flux.shape[0])
    weighted = weight_rows(own_phasors, intensity)
    total_stations = stations_local * groups
    channels = freq_ratio.shape[0]
    columns = jnp.einsum(
        "ack,nck->can",
        weighted,
        make_phasors(
            lax.all_gather(station_rows, "stn", axis=0, tiled=True),
            lax.all_gather(iono_phase, "stn", axis=0, tiled=True),
            directions,
            freq_ratio,
        ),
        preferred_element_type=jnp.float32,
    )
    visible = columns.reshape(channels, 2, stations_local, total_stations)
    first_row = lax.axis_index("stn") * stations_local
    rows_global = first_row + jnp.arange(stations_local, dtype=jnp.int32)
    cross_only = rows_global[:, None] != jnp.arange(total_stations, dtype=jnp.int32)[None, :]
    return jnp.where(cross_only[None, None], visible, jnp.zeros_like(visible))


def solution(mesh):
    in_specs = (
        P("stn", None, None),
        P(None, "stn", "chan", None, None),
        P("stn", "chan", None, None),
        P(None, "stn"),
        P(),
        P("chan"),
        P(),
        P(),
    )
    out_specs = P("chan", None, "stn", None)
    return jax.shard_map(body, mesh=mesh, in_specs=in_specs, out_specs=out_specs, check_vma=False)
```

profile of v0, /device:TPU:0, one launch (start us, length us, event | category | flops | bytes accessed | tf_op | source)
XLA Modules:
  0.0 576.7 jit_solution(3012017053386605129)
XLA Ops:
  0.0 1.7 copy.15
  1.7 7.4 %all-to-all-start = ((f32[2,16,1024]{2,0,1:T(2,128)}), f32[2,16,1024]{2,0,1:T(2,128)S(1)}, u32[]{:S(2)}, u32[]{:S(2)}) async-start(f32[2,16,1024]{2,0,1:T(2,128)} %bitcast.74), calls=%async_computation | async-start | bytes 262144 | tf_op jit(solution)/shard_map/all_to_all | solution.py:72
  9.1 0.9 copy.12
  10.0 0.1 compare_select_fusion.4
  10.0 0.8 fusion.17
  10.9 22.0 %all-gather = f32[16,16,3]{1,2,0:T(4,128)S(1)} all-gather(f32[1,16,3]{1,2,0:T(4,128)} %bitcast.98), channel_id=1, replica_groups=mesh['stn'=16,'chan'=2] {'stn'}, dimensions={0}, use_global_device_ids=true | all-gather | bytes 3264 | tf_op jit(solution)/shard_map/all_gather | solution.py:95
  32.9 0.1 reshape.551
  33.0 0.7 fusion.19
  33.6 0.8 slice_bitcast_fusion.2
  34.4 0.8 multiply_multiply_fusion
  35.2 0.1 multiply_add_fusion.3
  35.3 2.1 copy.13
  37.5 0.2 multiply_add_fusion
  37.6 0.0 all-to-all-done
  37.6 0.3 compare_select_fusion.3
  37.9 0.2 compare_select_fusion.2
  38.2 90.5 %gather_fusion.3 = f32[16384]{0:T(1024)S(1)} fusion(f32[524288]{0:T(1024)S(1)} %bitcast.75, s32[16384]{0:T(1024)S(1)} %broadcast_clamp_fusion), kind=kCustom, calls=%fused_computation.3 | custom fusion | bytes 196608 | tf_op jit(solution)/shard_map/gather | solution.py:19
  128.8 90.5 %gather_fusion.2 = f32[16384]{0:T(1024)S(1)} fusion(f32[524288]{0:T(1024)S(1)} %bitcast.76, s32[16384]{0:T(1024)S(1)} %broadcast_clamp_fusion.1), kind=kCustom, calls=%fused_computation.2 | custom fusion | bytes 196608 | tf_op jit(solution)/shard_map/gather | solution.py:19
  219.3 90.5 %gather_fusion.1 = f32[16384]{0:T(1024)S(1)} fusion(f32[524288]{0:T(1024)S(1)} %bitcast.77, s32[16384]{0:T(1024)S(1)} %broadcast_clamp_fusion.2), kind=kCustom, calls=%fused_computation.1 | custom fusion | bytes 196608 | tf_op jit(solution)/shard_map/gather | solution.py:18
  309.9 0.0 copy-start
  309.9 90.5 %gather_fusion = f32[16384]{0:T(1024)S(1)} fusion(f32[524288]{0:T(1024)S(1)} %bitcast.78, s32[16384]{0:T(1024)S(1)} %broadcast_clamp_fusion.3), kind=kCustom, calls=%fused_computation | custom fusion | bytes 196608 | tf_op jit(solution)/shard_map/gather | solution.py:18
  400.4 1.0 multiply_add_fusion.2
  401.4 3.5 all-to-all-start.1
  404.9 0.1 iota_compare_fusion
  405.0 6.8 %all-to-all-done.1 = f32[16,1,1024]{2,1,0:T(1,128)S(1)} async-done(((f32[16,1,1024]{2,1,0:T(1,128)}), f32[16,1,1024]{2,1,0:T(1,128)S(1)}, u32[]{:S(2)}, u32[]{:S(2)}) %all-to-all-start.1) | async-done | bytes 65568 | tf_op jit(solution)/shard_map/all_to_all | solution.py:76
  411.8 60.4 %scatter_custom_fusion = f32[4097]{0:T(1024)S(1)} fusion(s32[16384]{0:T(1024)S(1)} %bitcast.90, f32[16384]{0:T(1024)S(1)} %bitcast.91, f32[]{:T(128)} %constant.11.clone.1), kind=kCustom, calls=%fused_computation.55 | custom fusion | bytes 16392 | tf_op jit(solution)/shard_map/scatter | solution.py:81
  472.2 4.4 all_gather.9
  476.6 19.4 %all_gather.11 = f32[256,512]{1,0:T(8,128)S(1)} all-gather(f32[16,512]{1,0:T(8,128)S(1)} %all_gather.9), channel_id=1, replica_groups=mesh['stn'=16,'chan'=2] {'stn'}, dimensions={0}, use_global_device_ids=true | all-gather | bytes 557056 | tf_op jit(solution)/shard_map/all_gather | solution.py:96
  496.0 0.0 copy-done
  496.0 3.9 fusion.16
  499.9 4.3 multiply_convert_fusion.1
  504.2 62.5 %cosine_convert_fusion = (bf16[256,32,512]{2,0,1:T(8,128)(2,1)}, bf16[256,32,512]{2,0,1:T(8,128)(2,1)}) fusion(f32[32]{0:T(128)S(1)} %copy-done, f32[256,512]{1,0:T(8,128)S(1)} %all_gather.11, f32[256,512]{1,0:T(8,128)S(1)} %multiply_add_fusion, f32[32]{0:T(128)S(1)} %get-tuple-element.24), kind=kLoop, calls=%fused_computation.11 | loop fusion | flops 20971520 | bytes 17826048 | tf_op jit(solution)/shard_map/convert
  566.6 8.9 %fusion = f32[32,32,256]{2,1,0:T(8,128)S(1)} fusion(bf16[256,32,512]{2,0,1:T(8,128)(2,1)} %get-tuple-element.8, bf16[256,32,512]{2,0,1:T(8,128)(2,1)} %get-tuple-element.7, bf16[16,32,512]{2,0,1:T(8,128)(2,1)S(1)} %fusion.16, bf16[16,32,512]{2,0,1:T(8,128)(2,1)S(1)} %get-tuple-element.10, bf16[16,32,512]{2,0,1:T(8,128)(2,1)S(1)} %get-tuple-element.9), kind=kOutput, calls=%fused_computation.6 | convolution fusion | flops 578813952 | bytes 19398656 | tf_op jit(solution)/shard_map/ack,nck->can/dot_general | solution.py:91
  575.5 1.1 broadcast_select_fusion
  (9 shorter events, 0.1 us)
Async XLA Ops:
  1.7 36.0 %all-to-all-start = ((f32[2,16,1024]{2,0,1:T(2,128)}), f32[2,16,1024]{2,0,1:T(2,128)S(1)}, u32[]{:S(2)}, u32[]{:S(2)}) async-start(f32[2,16,1024]{2,0,1:T(2,128)} %bitcast.74), calls=%async_computation | async-start | bytes 262144 | tf_op jit(solution)/shard_map/all_to_all | solution.py:72
  309.9 186.1 %copy-start = (f32[32]{0:T(128)S(1)}, f32[32]{0:T(128)}, u32[]{:S(2)}) copy-start(f32[32]{0:T(128)} %param.13) | copy-start | bytes 388
  401.4 10.4 %all-to-all-start.1 = ((f32[16,1,1024]{2,1,0:T(1,128)}), f32[16,1,1024]{2,1,0:T(1,128)S(1)}, u32[]{:S(2)}, u32[]{:S(2)}) async-start(f32[16,1,1024]{2,1,0:T(1,128)} %multiply_add_fusion.2), calls=%async_computation.1 | async-start | bytes 131072 | tf_op jit(solution)/shard_map/all_to_all | solution.py:76
where the time goes:
time: 577 us
  local copies, waits for them, and re-layouts  429 us (74%)
  other arithmetic  75.1 us (13%)
  blocking collectives  45.8 us (8%)
  starting transfers between devices  10.9 us (2%)
  matrix products  8.92 us (2%)
  waiting for transfers between devices  6.79 us (1%)
    gather x2, local copies, waits for them, and re-layouts, interpolate(): lower_pair = (1.0 - frac_x) * values[corner] + frac_x * values[corner + 1]  181 us
    gather x1, local copies, waits for them, and re-layouts, interpolate(): values[corner + tile_cols + 1]  90.5 us
    gather x1, local copies, waits for them, and re-layouts, interpolate(): values[corner + tile_cols]  90.5 us
    another operation x1, other arithmetic  62.5 us
    scatter x1, local copies, waits for them, and re-layouts, body(): jnp.zeros((queries + 1,), jnp.float32).at[query_dest.reshape(-1)]  60.4 us
    all_gather x1, blocking collectives, body(): lax.all_gather(station_rows, 'stn', axis=0, tiled=True)  22 us
    all_gather x1, blocking collectives, body(): lax.all_gather(iono_phase, 'stn', axis=0, tiled=True)  19.4 us
  transfers between devices with their start and end apart: 2, of which 1 were waited for; matrix products, arithmetic and copies ran while one was open for 1% of the time, Pallas kernels for 0%

commit v1 on v0

--- a/solution.py
+++ b/solution.py
@@ -5,6 +5,32 @@
 from jax.sharding import PartitionSpec as P
 
 TWO_PI = 2.0 * math.pi
+
+
+def clear_forms(block_here):
+    near = jax.lax.axis_size("stn")
+    field_out = jax.lax.axis_index("stn")
+    t1, inter, oldest = (near, field_out, block_here.shape[0])
+    block_next = lax.dynamic_update_slice_in_dim(
+        jnp.zeros(
+            [t * t1 if j == 0 else t for j, t in enumerate(block_here.shape)], block_here.dtype
+        ),
+        block_here,
+        inter * oldest,
+        axis=0,
+    )
+    frame_out = local_now = block_here
+    for nth in range(1, t1 // 2 + 1):
+        frame_out = jax.lax.ppermute(frame_out, "stn", [(j, (j + 1) % t1) for j in range(t1)])
+        block_next = lax.dynamic_update_slice_in_dim(
+            block_next, frame_out, (inter - nth) % t1 * oldest, axis=0
+        )
+        if 2 * nth < t1:
+            local_now = jax.lax.ppermute(local_now, "stn", [(j, (j - 1) % t1) for j in range(t1)])
+            block_next = lax.dynamic_update_slice_in_dim(
+                block_next, local_now, (inter + nth) % t1 * oldest, axis=0
+            )
+    return block_next
 
 
 def interpolate(values, coords, strip_rows, tile_cols):
@@ -92,7 +118,7 @@
         "ack,nck->can",
         weighted,
         make_phasors(
-            lax.all_gather(station_rows, "stn", axis=0, tiled=True),
+            clear_forms(station_rows),
             lax.all_gather(iono_phase, "stn", axis=0, tiled=True),
             directions,
             freq_ratio,

time: 577 us -> 598 us (1.036)
  starting transfers between devices: 10.9 us -> 39.2 us
  blocking collectives: 45.8 us -> 23.8 us
  waiting for transfers between devices: 6.79 us -> 17.1 us
    ppermute x0 -> x15, starting transfers between devices: none -> 32 us  [the longest x7 30.9 us: clear_forms(): jax.lax.ppermute(local_now, 'stn', [(j, (j - 1) % t1) for j in range(t1)])]
    all_gather x1 -> x0, blocking collectives: 22 us -> none  [body(): lax.all_gather(station_rows, 'stn', axis=0, tiled=True)]
    ppermute x0 -> x15, waiting for transfers between devices: none -> 10.5 us  [the longest x8 10 us: clear_forms(): jax.lax.ppermute(frame_out, 'stn', [(j, (j + 1) % t1) for j in range(t1)])]
  transfers between devices with their start and end apart: 2 -> 17, of which waited for: 1 -> 13; matrix products, arithmetic and copies ran while one was open for 1% -> 2% of each run, Pallas kernels for 0% -> 0%
where the time goes in v1:
time: 598 us; the launch traced here: 597 us
  local copies, waits for them, and re-layouts  433 us (72%)
  other arithmetic  75.2 us (13%)
  starting transfers between devices  39.2 us (7%)
  blocking collectives  23.8 us (4%)
  waiting for transfers between devices  17.1 us (3%)
  matrix products  8.91 us (1%)
    gather x2, local copies, waits for them, and re-layouts, interpolate(): lower_pair = (1.0 - frac_x) * values[corner] + frac_x * values[corner + 1]  181 us
    gather x1, local copies, waits for them, and re-layouts, interpolate(): values[corner + tile_cols + 1]  90.5 us
    gather x1, local copies, waits for them, and re-layouts, interpolate(): values[corner + tile_cols]  90.5 us
    another operation x1, other arithmetic  62.5 us
    scatter x1, local copies, waits for them, and re-layouts, body(): jnp.zeros((queries + 1,), jnp.float32).at[query_dest.reshape(-1)]  60.4 us
    ppermute x7, starting transfers between devices, clear_forms(): jax.lax.ppermute(local_now, 'stn', [(j, (j - 1) % t1) for j in range(t1)])  30.9 us
    all_gather x1, blocking collectives, body(): lax.all_gather(iono_phase, 'stn', axis=0, tiled=True)  19.4 us
  transfers between devices with their start and end apart: 17, of which 13 were waited for; matrix products, arithmetic and copies ran while one was open for 2% of the time, Pallas kernels for 0%

profile of v1, /device:TPU:0, one launch (start us, length us, event | category | flops | bytes accessed | tf_op | source)
XLA Modules:
  0.0 597.4 jit_solution(17344677377557127902)
XLA Ops:
  0.0 0.5 collective-permute-start
  0.5 5.0 collective-permute-start.1
  5.4 1.7 copy.13
  7.1 3.7 all-to-all-start
  10.8 0.8 slice_bitcast_fusion.2
  11.6 0.8 fusion.17
  12.4 0.9 copy.10
  13.4 0.7 fusion.19
  14.1 0.8 multiply_multiply_fusion
  14.9 0.1 multiply_add_fusion.3
  14.9 0.1 iota_compare_fusion
  15.2 2.1 copy.11
  17.4 0.8 dynamic_update_slice.48
  18.3 0.6 collective-permute-start.2
  18.8 4.0 collective-permute-start.3
  22.8 0.2 dynamic_update_slice.49
  23.0 0.2 dynamic_update_slice.50
  23.2 0.8 collective-permute-done.2
  24.0 0.1 collective-permute-done.3
  24.1 4.4 collective-permute-start.5
  28.5 0.2 dynamic_update_slice.51
  28.7 0.2 dynamic_update_slice.52
  28.9 0.8 collective-permute-done.4
  29.7 0.1 collective-permute-done.5
  29.8 4.4 collective-permute-start.7
  34.2 0.2 dynamic_update_slice.53
  34.4 0.2 dynamic_update_slice.54
  34.6 0.8 collective-permute-done.6
  35.4 0.1 collective-permute-done.7
  35.5 4.4 collective-permute-start.9
  39.9 0.2 dynamic_update_slice.55
  40.1 0.2 dynamic_update_slice.56
  40.3 0.8 collective-permute-done.8
  41.2 0.1 collective-permute-done.9
  41.2 4.4 collective-permute-start.11
  45.6 0.2 dynamic_update_slice.57
  45.8 0.2 dynamic_update_slice.58
  46.1 0.8 collective-permute-done.10
  46.9 0.1 collective-permute-done.11
  46.9 4.4 collective-permute-start.13
  51.3 0.2 dynamic_update_slice.59
  51.5 0.2 dynamic_update_slice.60
  51.8 0.8 collective-permute-done.12
  52.6 0.2 dynamic_update_slice.61
  52.8 0.3 dynamic_update_slice.62
  53.0 5.2 collective-permute-done.14
  58.4 0.3 compare_select_fusion.3
  58.7 0.2 compare_select_fusion.2
  58.9 90.5 %gather_fusion.1 = f32[16384]{0:T(1024)S(1)} fusion(f32[524288]{0:T(1024)S(1)} %bitcast.71, s32[16384]{0:T(1024)S(1)} %broadcast_clamp_fusion.2), kind=kCustom, calls=%fused_computation.1 | custom fusion | bytes 196608 | tf_op jit(solution)/shard_map/gather | solution.py:44
  149.5 90.5 %gather_fusion.2 = f32[16384]{0:T(1024)S(1)} fusion(f32[524288]{0:T(1024)S(1)} %bitcast.72, s32[16384]{0:T(1024)S(1)} %broadcast_clamp_fusion.1), kind=kCustom, calls=%fused_computation.2 | custom fusion | bytes 196608 | tf_op jit(solution)/shard_map/gather | solution.py:45
  240.0 90.5 %gather_fusion.3 = f32[16384]{0:T(1024)S(1)} fusion(f32[524288]{0:T(1024)S(1)} %bitcast.73, s32[16384]{0:T(1024)S(1)} %broadcast_clamp_fusion), kind=kCustom, calls=%fused_computation.3 | custom fusion | bytes 196608 | tf_op jit(solution)/shard_map/gather | solution.py:45
  330.6 90.5 %gather_fusion = f32[16384]{0:T(1024)S(1)} fusion(f32[524288]{0:T(1024)S(1)} %bitcast.74, s32[16384]{0:T(1024)S(1)} %broadcast_clamp_fusion.3), kind=kCustom, calls=%fused_computation | custom fusion | bytes 196608 | tf_op jit(solution)/shard_map/gather | solution.py:44
  421.2 1.0 multiply_add_fusion.2
  422.2 3.5 all-to-all-start.1
  425.7 0.2 multiply_add_fusion
  425.8 6.7 %all-to-all-done.1 = f32[16,1,1024]{2,1,0:T(1,128)S(1)} async-done(((f32[16,1,1024]{2,1,0:T(1,128)}), f32[16,1,1024]{2,1,0:T(1,128)S(1)}, u32[]{:S(2)}, u32[]{:S(2)}) %all-to-all-start.1) | async-done | bytes 65568 | tf_op jit(solution)/shard_map/all_to_all | solution.py:102
  432.5 60.4 %scatter_custom_fusion = f32[4097]{0:T(1024)S(1)} fusion(s32[16384]{0:T(1024)S(1)} %bitcast.86, f32[16384]{0:T(1024)S(1)} %bitcast.87, f32[]{:T(128)} %constant.114.clone.1), kind=kCustom, calls=%fused_computation.55 | custom fusion | bytes 16392 | tf_op jit(solution)/shard_map/scatter | solution.py:107
  492.9 4.4 all_gather.6
  497.3 19.4 %all_gather.7 = f32[256,512]{1,0:T(8,128)S(1)} all-gather(f32[16,512]{1,0:T(8,128)S(1)} %all_gather.6), channel_id=1, replica_groups=mesh['stn'=16,'chan'=2] {'stn'}, dimensions={0}, use_global_device_ids=true | all-gather | bytes 557056 | tf_op jit(solution)/shard_map/all_gather | solution.py:122
  516.7 4.2 multiply_convert_fusion.1
  520.9 3.9 fusion.16
  524.9 62.5 %cosine_convert_fusion = (bf16[256,32,512]{2,0,1:T(8,128)(2,1)}, bf16[256,32,512]{2,0,1:T(8,128)(2,1)}) fusion(f32[32]{0:T(128)S(1)} %copy-done, f32[256,512]{1,0:T(8,128)S(1)} %all_gather.7, f32[256,512]{1,0:T(8,128)S(1)} %multiply_add_fusion, f32[32]{0:T(128)S(1)} %get-tuple-element.24), kind=kLoop, calls=%fused_computation.11 | loop fusion | flops 20971520 | bytes 17826048 | tf_op jit(solution)/shard_map/convert
  587.4 8.9 %fusion = f32[32,32,256]{2,1,0:T(8,128)S(1)} fusion(bf16[256,32,512]{2,0,1:T(8,128)(2,1)} %get-tuple-element.8, bf16[256,32,512]{2,0,1:T(8,128)(2,1)} %get-tuple-element.7, bf16[16,32,512]{2,0,1:T(8,128)(2,1)S(1)} %fusion.16, bf16[16,32,512]{2,0,1:T(8,128)(2,1)S(1)} %get-tuple-element.10, bf16[16,32,512]{2,0,1:T(8,128)(2,1)S(1)} %get-tuple-element.9), kind=kOutput, calls=%fused_computation.6 | convolution fusion | flops 578813952 | bytes 19398656 | tf_op jit(solution)/shard_map/ack,nck->can/dot_general | solution.py:117
  596.3 1.1 broadcast_select_fusion
  (23 shorter events, 0.2 us)
Async XLA Ops:
  0.0 18.3 %collective-permute-start = (f32[16,3]{0,1:T(4,128)}, f32[16,3]{0,1:T(4,128)S(1)}, u32[]{:S(2)}, u32[]{:S(2)}) collective-permute-start(f32[16,3]{0,1:T(4,128)} %bitcast.94), channel_id=1, source_target_pairs={{0,2},{2,4},{4,6},{6,8},{8,10},{10,12},{12,14},{14,16},{16,18},{18... | collective-permute-start | bytes 584 | tf_op jit(solution)/shard_map/ppermute | solution.py:24
  0.5 18.3 %collective-permute-start.1 = (f32[16,3]{0,1:T(4,128)}, f32[16,3]{0,1:T(4,128)S(1)}, u32[]{:S(2)}, u32[]{:S(2)}) collective-permute-start(f32[16,3]{0,1:T(4,128)} %bitcast.95), channel_id=1, source_target_pairs={{0,30},{2,0},{4,2},{6,4},{8,6},{10,8},{12,10},{14,12},{16,14},{18,... | collective-permute-start | bytes 584 | tf_op jit(solution)/shard_map/ppermute | solution.py:29
  7.1 51.3 %all-to-all-start = ((f32[2,16,1024]{2,0,1:T(2,128)}), f32[2,16,1024]{2,0,1:T(2,128)S(1)}, u32[]{:S(2)}, u32[]{:S(2)}) async-start(f32[2,16,1024]{2,0,1:T(2,128)} %bitcast.70), calls=%async_computation | async-start | bytes 262144 | tf_op jit(solution)/shard_map/all_to_all | solution.py:98
  18.3 5.8 collective-permute-start.2
  18.8 5.3 collective-permute-start.3
  24.0 5.7 collective-permute-start.4
  24.1 5.7 collective-permute-start.5
  29.7 5.7 collective-permute-start.6
  29.8 5.7 collective-permute-start.7
  35.4 5.7 collective-permute-start.8
  35.5 5.7 collective-permute-start.9
  41.1 5.7 collective-permute-start.10
  41.2 5.7 collective-permute-start.11
  46.9 5.7 collective-permute-start.12
  46.9 5.8 collective-permute-start.13
  52.6 5.7 collective-permute-start.14
  330.6 186.1 %copy-start = (f32[32]{0:T(128)S(1)}, f32[32]{0:T(128)}, u32[]{:S(2)}) copy-start(f32[32]{0:T(128)} %param.13) | copy-start | bytes 388
  422.2 10.4 %all-to-all-start.1 = ((f32[16,1,1024]{2,1,0:T(1,128)}), f32[16,1,1024]{2,1,0:T(1,128)S(1)}, u32[]{:S(2)}, u32[]{:S(2)}) async-start(f32[16,1,1024]{2,1,0:T(1,128)} %multiply_add_fusion.2), calls=%async_computation.1 | async-start | bytes 131072 | tf_op jit(solution)/shard_map/all_to_all | solution.py:102
